TPU v7x, 32 devices: a whole 2x2x4 slice. The times are simulated.
32 devices in a mesh: gx: 8 (over y, x, core), gy: 4 (over z).
Axes of the slice: x: 2, y: 2, z: 4, core: 2. Of those that a mesh axis runs over, the one named last changes fastest.
Arguments:
- temp_start: float32 [8, 1024, 2048], P(None, ('gx', 'gy')), may hold values from -6 to 6
- heat_input: float32 [8, 1024, 2048], P(None, ('gx', 'gy')), may hold values from -3 to 3
- lateral: float32 [8], replicated, may hold values from 0.03 to 0.15
- vertical: float32 [7], replicated, may hold values from 0.03 to 0.15
- weighting: float32 [8], replicated, may hold values from -1 to 1
- modulus: float32 [1024, 2048], P('gx', 'gy'), may hold values from 0.3 to 3
- warp_prev: float32 [1024, 2048], P('gx', 'gy'), may hold values from -6 to 6
- joint_cell: int32 [65536], P(('gx', 'gy')), may hold values from 0 to 65535
- joint_owner: int32 [65536, 1], P(('gx', 'gy')), may hold values from 0 to 31; in each aligned block of 2048 rows (0 to 2047, 2048 to 4095, ...) at most 192 rows name the same one
- joint_strain: float32 [2, 32, 6144], P(None, ('gx', 'gy')), may hold values from -4 to 4
- joint_resist: float32 [32, 6144], P(('gx', 'gy')), may hold values from 1 to 2
Outputs:
- warpage: float32 [1024, 2048], P('gx', 'gy')
- strain_next: float32 [2, 32, 6144], P(None, ('gx', 'gy'))
- resist_next: float32 [32, 6144], P(('gx', 'gy'))
Inputs may be any that keep to these rules, and one draw needn't show every extreme that they name: `joint_owner`: among the 2048 joints of one device at most 192 have the same owner, and on some device exactly 192 do.
All inputs are finite; a program needn't handle non-finite values.
Results may differ from a plain program's by a relative error of at most 0.0003.
Values sent between devices are 32-bit elements; how exact they have to be, the bound alone decides.
No kernel may reach another device: no remote copies, remote signals or barrier semaphores. Data moves between devices by JAX's collectives and lax.ppermute only.
A program may use at most 320 MiB of HBM per device.

v0:
```python
import jax
import jax.numpy as jnp
from jax import lax
from jax.sharding import PartitionSpec as P

STEPS = 2
SWEEPS = 3
stiffness = 0.2
shear_mod = 0.6
rate_scale = 0.5
sat_level = 2.5
sat_power = 0.3
harden = 2.0
FLAT = ("gx", "gy")


def exchange(last, leading, axis):
    count = lax.axis_size(axis)
    up = [(i, i + 1) for i in range(count - 1)]
    down = [(j, i) for i, j in up]
    return (lax.ppermute(last, axis, up), lax.ppermute(leading, axis, down))


def with_halo(array, sides, width):
    for axis, dim in sides:
        length = array.shape[dim]
        last = lax.slice_in_dim(array, length - width, length, axis=dim)
        leading = lax.slice_in_dim(array, 0, width, axis=dim)
        before, after = exchange(last, leading, axis)
        array = jnp.concatenate([before, array, after], axis=dim)
    return array


def thermal_step(ext, heat_rows, lateral, vertical):
    cols = jnp.pad(ext, ((0, 0), (0, 0), (1, 1)))
    center = ext[:, 1:-1]
    lap = ext[:, 2:] + ext[:, :-2] + cols[:, 1:-1, 2:] + cols[:, 1:-1, :-2] - 4.0 * center
    flux = vertical[:, None, None] * (center[1:] - center[:-1])
    vert = jnp.pad(flux, ((0, 1), (0, 0), (0, 0))) - jnp.pad(flux, ((1, 0), (0, 0), (0, 0)))
    return center + lateral[:, None, None] * lap + vert + heat_rows


def moment_of(field, weighting):
    total = weighting[0] * field[0]
    for layer in range(1, field.shape[0]):
        total = total + weighting[layer] * field[layer]
    return total


def sweep(w_pad, e_pad, load):
    center = e_pad[1:-1, 1:-1]
    e_up = 0.5 * (center + e_pad[:-2, 1:-1])
    e_down = 0.5 * (center + e_pad[2:, 1:-1])
    e_left = 0.5 * (center + e_pad[1:-1, :-2])
    e_right = 0.5 * (center + e_pad[1:-1, 2:])
    numer = (
        load
        + e_up * w_pad[:-2, 1:-1]
        + e_down * w_pad[2:, 1:-1]
        + e_left * w_pad[1:-1, :-2]
        + e_right * w_pad[1:-1, 2:]
    )
    denom = stiffness + e_up + e_down + e_left + e_right
    return numer / denom


def anand(strain, resist, recv):
    total, inelastic = (strain[0], strain[1])
    increment, theta, live = (recv[0], recv[1], recv[2])
    total_new = total + increment
    arrhen = jnp.exp(2.0 - 2.0 / (1.0 + 0.1 * theta * theta))
    hyper = jnp.sinh(shear_mod * (total_new - inelastic) / resist)
    rate = rate_scale * arrhen * hyper * jnp.abs(hyper)
    inelastic_new = inelastic + rate
    target = sat_level * jnp.power(1.0 + jnp.abs(rate) / arrhen, sat_power)
    resist_new = resist + harden * (1.0 - resist / target) * jnp.abs(rate)
    keep = live > 0.5
    strain_out = jnp.stack(
        [jnp.where(keep, total_new, total), jnp.where(keep, inelastic_new, inelastic)]
    )
    return (strain_out, jnp.where(keep, resist_new, resist))


def thermal(temp, heat, lateral, vertical):
    devices = lax.axis_size(FLAT)
    t = lax.axis_index(FLAT)
    rows = temp.shape[1]
    h = STEPS
    last = jnp.concatenate([temp[:, rows - h :], heat[:, rows - (h - 1) :]], axis=1)
    leading = jnp.concatenate([temp[:, :h], heat[:, : h - 1]], axis=1)
    before, after = exchange(last, leading, FLAT)
    ext = jnp.concatenate([before[:, :h], temp, after[:, :h]], axis=1)
    heat_ext = jnp.concatenate([before[:, h:], heat, after[:, h:]], axis=1)
    for step in range(1, STEPS + 1):
        r = STEPS - step
        heat_rows = heat_ext[:, h - 1 - r : h - 1 - r + rows + 2 * r]
        ext = thermal_step(ext, heat_rows, lateral, vertical)
        if r > 0:
            g = t * rows + jnp.arange(-r, rows + r)
            inside = (g >= 0) & (g < devices * rows)
            ext = jnp.where(inside[None, :, None], ext, 0.0)
    return ext


def relay(load, top, width):
    n_gy = lax.axis_size("gy")
    rows, cols = load.shape
    cm = cols // n_gy
    before, after = exchange(load[rows - width :], load[:width], FLAT)
    load_ext = jnp.concatenate([before, load, after], axis=0)
    lp = jnp.pad(load_ext, ((0, 0), (width, width)))
    tp = jnp.pad(top, ((width, width), (width, width)))
    both = jnp.stack([lp, tp])
    send = jnp.stack([both[:, :, k * cm : k * cm + cm + 2 * width] for k in range(n_gy)])
    recv = lax.all_to_all(send, "gy", split_axis=0, concat_axis=0, tiled=True)
    parts = []
    for k in range(n_gy):
        lo = 0 if k == 0 else width
        hi = rows + 2 * width if k == n_gy - 1 else rows + width
        parts.append(recv[k, 0, lo:hi])
    load_m = jnp.concatenate(parts, axis=0)
    top_m = jnp.concatenate(
        [recv[k, 1, width : rows + width, width : cm + width] for k in range(n_gy)], axis=0
    )
    return (load_m, top_m)


def joint_ranks(owners, devices):
    count = owners.shape[0]
    block = 128 if count % 128 == 0 else count
    nb = count // block
    onehot = (owners[:, None] == jnp.arange(devices, dtype=jnp.int32)[None, :]).astype(jnp.float32)
    oh = onehot.reshape(nb, block, devices)
    ar = jnp.arange(block)
    tri = (ar[:, None] >= ar[None, :]).astype(jnp.float32)
    within = jnp.einsum("ij,bjd->bid", tri, oh, precision=lax.Precision.HIGHEST)
    totals = within[:, -1, :]
    ab = jnp.arange(nb)
    stri = (ab[:, None] > ab[None, :]).astype(jnp.float32)
    offs = jnp.dot(stri, totals, precision=lax.Precision.HIGHEST)
    cum = (within + offs[:, None, :]).reshape(count, devices)
    return jnp.sum(cum * onehot, axis=1).astype(jnp.int32) - 1


def body(
    temp_start,
    heat_input,
    lateral,
    vertical,
    weighting,
    modulus,
    warp_prev,
    joint_cell,
    joint_owner,
    joint_strain,
    joint_resist,
):
    devices = lax.axis_size(FLAT)
    n_gx, n_gy = (lax.axis_size("gx"), lax.axis_size("gy"))
    gi, gj = (lax.axis_index("gx"), lax.axis_index("gy"))
    rm, cm = warp_prev.shape
    wm = with_halo(jnp.stack([warp_prev, modulus]), (("gx", 1), ("gy", 2)), SWEEPS)
    owners = joint_owner[:, 0]
    capacity = joint_resist.shape[1] // devices
    slots = owners * capacity + joint_ranks(owners, devices)
    temp = thermal(temp_start, heat_input, lateral, vertical)
    load_t = moment_of(temp, weighting)
    load, top = relay(load_t, temp[-1], SWEEPS - 1)
    warp = wm[0]
    mod_ext = wm[1]
    for step in range(1, SWEEPS + 1):
        r = SWEEPS - step
        off = SWEEPS - (r + 1)
        e_pad = mod_ext[off : off + rm + 2 * r + 2, off : off + cm + 2 * r + 2]
        lo = SWEEPS - 1 - r
        ld = load[lo : lo + rm + 2 * r, lo : lo + cm + 2 * r]
        warp = sweep(warp, e_pad, ld)
        if r > 0:
            gr = gi * rm + jnp.arange(-r, rm + r)
            gc = gj * cm + jnp.arange(-r, cm + r)
            inside = ((gr >= 0) & (gr < n_gx * rm))[:, None] & ((gc >= 0) & (gc < n_gy * cm))[
                None, :
            ]
            warp = jnp.where(inside, warp, 0.0)
    fields = jnp.stack([(warp - warp_prev).reshape(-1), top.reshape(-1)])
    picked = fields[:, joint_cell]
    values = jnp.concatenate([picked, jnp.ones_like(picked[:1])], axis=0)
    outgoing = jnp.zeros((3, devices * capacity), jnp.float32).at[:, slots].set(values)
    incoming = lax.all_to_all(outgoing, FLAT, split_axis=1, concat_axis=1, tiled=True)
    strain_next, resist_next = anand(joint_strain, joint_resist, incoming[:, None, :])
    return (warp, strain_next, resist_next)


def solution(mesh):
    return jax.shard_map(
        body,
        mesh=mesh,
        in_specs=(
            P(None, FLAT, None),
            P(None, FLAT, None),
            P(),
            P(),
            P(),
            P("gx", "gy"),
            P("gx", "gy"),
            P(FLAT),
            P(FLAT, None),
            P(None, FLAT, None),
            P(FLAT, None),
        ),
        out_specs=(P("gx", "gy"), P(None, FLAT, None), P(FLAT, None)),
        check_vma=False,
    )
```

profile of v0, /device:TPU:0, one launch (start us, length us, event | category | flops | bytes accessed | tf_op | source)
XLA Modules:
  0.0 136.8 jit_solution(4110263155972718763)
XLA Ops:
  0.7 1.4 %fusion.88 = (f32[8,2,2048]{2,1,0:T(2,128)S(1)}, f32[8,2,2048]{2,1,0:T(2,128)S(1)}) fusion(f32[8,32,2048]{2,1,0:T(8,128)} %param.11), kind=kLoop, calls=%fused_computation.191 | loop fusion | bytes 524288 | tf_op jit(solution)/shard_map/slice | solution.py:89
  2.1 1.3 fusion.89
  3.5 5.0 %collective-permute-start = (f32[8,3,2048]{2,1,0:T(4,128)S(1)}, f32[8,3,2048]{2,1,0:T(4,128)S(1)}, u32[]{:S(2)}, u32[]{:S(2)}) collective-permute-start(f32[8,3,2048]{2,1,0:T(4,128)S(1)} %pad_maximum_fusion.5), channel_id=1, source_target_pairs={{0,1},{1,2},{2,3},{3,4},{4,5},{5,6},{6,7},{7,8},{8,9},{9,10},{10,1... | collective-permute-start | bytes 589832 | tf_op jit(solution)/shard_map/ppermute | solution.py:21
  8.6 1.3 collective-permute-start.1
  9.9 0.8 pad_maximum_fusion.14
  10.7 4.7 %collective-permute-start.4 = (f32[2,3,512]{2,1,0:T(4,128)S(1)}, f32[2,3,512]{2,1,0:T(4,128)S(1)}, u32[]{:S(2)}, u32[]{:S(2)}) collective-permute-start(f32[2,3,512]{2,1,0:T(4,128)S(1)} %get-tuple-element.31), channel_id=1, source_target_pairs={{0,4},{4,8},{8,12},{12,16},{16,20},{20,24},{24,28},{1,5},{5,9},{9,... | collective-permute-start | bytes 36872 | tf_op jit(solution)/shard_map/ppermute | solution.py:21
  15.4 1.3 collective-permute-start.5
  16.7 1.6 %fusion.94 = (f32[1]{0:T(128)}, f32[1]{0:T(128)}, f32[1]{0:T(128)}, f32[1]{0:T(128)}, f32[1]{0:T(128)}, /*index=5*/f32[1]{0:T(128)}, f32[1]{0:T(128)}, f32[1]{0:T(128)}) fusion(f32[8]{0:T(128)} %param.15), kind=kLoop, calls=%fused_computation.197 | loop fusion | bytes 64 | tf_op jit(solution)/shard_map/slice | solution.py:44
  18.3 0.9 convolution_bitcast_fusion
  19.9 3.4 %collective-permute-done.1 = f32[8,3,2048]{2,1,0:T(4,128)S(1)} collective-permute-done((f32[8,3,2048]{2,1,0:T(4,128)S(1)}, f32[8,3,2048]{2,1,0:T(4,128)S(1)}, u32[]{:S(2)}, u32[]{:S(2)}) %collective-permute-start.1) | collective-permute-done | bytes 196640 | tf_op jit(solution)/shard_map/ppermute | solution.py:21
  24.3 1.0 copy-done.1
  25.3 3.0 %fusion.7 = f32[8,34,2048]{2,1,0:T(8,128)S(1)} fusion(f32[8,36,2048]{2,1,0:T(8,128)S(1)} %pad_maximum_fusion, f32[8,2,2048]{2,1,0:T(2,128)S(1)} %slice.403, f32[8,32,2048]{2,1,0:T(8,128)S(1)} %copy-done, f32[8,2,2048]{2,1,0:T(2,128)S(1)} %slice.402, f32[8,1,2048]{2,1,0:T(1,128)S(1)} %slice.408, f32[8,32,2048]{2,1,0:T(8,128)S(1)} %copy-done.1, ...), kind=kLoop, calls=%fused_computation.13 | loop fusion | flops 8355840 | bytes 14353408 | tf_op jit(solution)/shard_map/jit(_where)/select_n | solution.py:101
  28.8 1.9 %fusion.15 = f32[8,32,2048]{2,1,0:T(8,128)S(1)} fusion(f32[8,32,2048]{2,1,0:T(8,128)S(1)} %copy-done.1, f32[8,34,2048]{2,1,0:T(8,128)S(1)} %fusion.7, f32[7,32,2048]{2,1,0:T(8,128)S(1)} %fusion.16, f32[8]{0:T(128)S(1)} %copy-done.9), kind=kLoop, calls=%fused_computation.24 | loop fusion | flops 5242880 | bytes 14942720 | tf_op jit(solution)/shard_map/add | solution.py:40
  30.7 5.2 %fusion.54 = f32[32,2048]{1,0:T(8,128)S(1)} fusion(f32[8,32,2048]{2,1,0:T(8,128)S(1)} %fusion.15, f32[]{:T(128)} %bitcast.8, f32[]{:T(128)} %bitcast.6, f32[]{:T(128)} %bitcast.5, f32[]{:T(128)} %bitcast.4, f32[]{:T(128)} %bitcast.3, f32[]{:T(128)} %bitcast.2, f32[]{:T(128)} %bitcast.1, f32[]{:T(128)} %bitcast), kind=kLoop, calls=%fused_computation.109 | loop fusion | flops 983040 | bytes 2359328 | tf_op jit(solution)/shard_map/add | solution.py:46
  35.9 2.5 %collective-permute-start.2 = (f32[2,2048]{1,0:T(2,128)S(1)}, f32[2,2048]{1,0:T(2,128)S(1)}, u32[]{:S(2)}, u32[]{:S(2)}) collective-permute-start(f32[2,2048]{1,0:T(2,128)S(1)} %get-tuple-element.33), channel_id=1, source_target_pairs={{0,1},{1,2},{2,3},{3,4},{4,5},{5,6},{6,7},{7,8},{8,9},{9,10},{10,1... | collective-permute-start | bytes 49160 | tf_op jit(solution)/shard_map/ppermute | solution.py:21
  38.4 1.3 collective-permute-start.3
  40.1 3.9 %collective-permute-done.3 = f32[2,2048]{1,0:T(2,128)S(1)} collective-permute-done((f32[2,2048]{1,0:T(2,128)S(1)}, f32[2,2048]{1,0:T(2,128)S(1)}, u32[]{:S(2)}, u32[]{:S(2)}) %collective-permute-start.3) | collective-permute-done | bytes 16416 | tf_op jit(solution)/shard_map/ppermute | solution.py:21
  45.3 1.2 pad_maximum_fusion.1
  46.5 5.4 %all-to-all-start = ((f32[4,2,36,516]{3,1,2,0:T(2,128)}), f32[4,2,36,516]{3,1,2,0:T(2,128)S(1)}, u32[]{:S(2)}, u32[]{:S(2)}) async-start(f32[4,2,36,516]{3,1,2,0:T(2,128)} %pad_maximum_fusion.1), calls=%async_computation | async-start | bytes 1474560 | tf_op jit(solution)/shard_map/all_to_all | solution.py:115
  52.1 3.9 %collective-permute-start.6 = (f32[2,134,3]{2,1,0:T(8,128)S(1)}, f32[2,134,3]{2,1,0:T(8,128)S(1)}, u32[]{:S(2)}, u32[]{:S(2)}) collective-permute-start(f32[2,134,3]{2,1,0:T(8,128)S(1)} %get-tuple-element.29), channel_id=1, source_target_pairs={{0,1},{1,2},{2,3},{4,5},{5,6},{6,7},{8,9},{9,10},{10,11},{12,13},{... | collective-permute-start | bytes 9656 | tf_op jit(solution)/shard_map/ppermute | solution.py:21
  56.0 1.5 %collective-permute-start.7 = (f32[2,134,3]{2,1,0:T(8,128)S(1)}, f32[2,134,3]{2,1,0:T(8,128)S(1)}, u32[]{:S(2)}, u32[]{:S(2)}) collective-permute-start(f32[2,134,3]{2,1,0:T(8,128)S(1)} %get-tuple-element.30), channel_id=1, source_target_pairs={{1,0},{2,1},{3,2},{5,4},{6,5},{7,6},{9,8},{10,9},{11,10},{13,12},{... | collective-permute-start | bytes 9656 | tf_op jit(solution)/shard_map/ppermute | solution.py:21
  57.5 9.2 %collective-permute-done.6 = f32[2,134,3]{2,1,0:T(8,128)S(1)} collective-permute-done((f32[2,134,3]{2,1,0:T(8,128)S(1)}, f32[2,134,3]{2,1,0:T(8,128)S(1)}, u32[]{:S(2)}, u32[]{:S(2)}) %collective-permute-start.6) | collective-permute-done | bytes 3248 | tf_op jit(solution)/shard_map/ppermute | solution.py:21
  67.1 4.3 %all-to-all-done = f32[4,2,36,516]{3,1,2,0:T(2,128)S(1)} async-done(((f32[4,2,36,516]{3,1,2,0:T(2,128)}), f32[4,2,36,516]{3,1,2,0:T(2,128)S(1)}, u32[]{:S(2)}, u32[]{:S(2)}) %all-to-all-start) | async-done | bytes 594464 | tf_op jit(solution)/shard_map/all_to_all | solution.py:115
  71.3 0.8 fusion.90
  73.5 0.9 fusion.23
  74.4 1.4 %subtract_bitcast_fusion = (f32[1,1,128,512]{3,2,1,0:T(8,128)S(1)}, f32[128,512]{1,0:T(8,128)}) fusion(f32[128,512]{1,0:T(8,128)S(1)} %copy-done.2, f32[130,514]{1,0:T(8,128)S(1)} %fusion.23, f32[134,518]{1,0:T(8,128)S(1)} %get-tuple-element.23, f32[132,516]{1,0:T(8,128)S(1)} %get-tuple-element.10), kind=kLoop, calls=%fused_computation.124 | loop fusion | flops 1441792 | bytes 3407872
  76.6 15.6 %copy.24 = f32[2,65536]{0,1:T(8,128)} copy(f32[2,65536]{1,0:T(2,128)S(1)} %pad_maximum_fusion.3) | data formatting | bytes 1048576 | tf_op jit(solution)/shard_map/stack | solution.py:185
  92.2 18.2 %gather_fusion = f32[2048,2]{1,0:T(8,128)} fusion(f32[2,65536]{0,1:T(8,128)} %copy.24, s32[2048]{0:T(1024)S(1)} %fusion.79), kind=kCustom, calls=%fused_computation | custom fusion | bytes 40960 | tf_op jit(solution)/shard_map/gather | solution.py:186
  110.4 6.8 %scatter_custom_fusion = f32[3,6144]{0,1:T(8,128)S(1)} fusion(s32[2048]{0:T(1024)S(1)} %bitcast.102, f32[]{:T(128)} %constant.34.clone.1, f32[2,2048]{0,1:T(8,128)} %bitcast.96, f32[]{:T(128)} %constant.45.clone.1), kind=kCustom, calls=%fused_computation.28 | custom fusion | bytes 90120 | tf_op jit(solution)/shard_map/scatter | solution.py:188
  117.2 1.5 %copy.25 = f32[3,32,192]{2,0,1:T(4,128)S(1)} copy(f32[3,32,192]{0,2,1:T(8,128)S(1)} %bitcast.89) | data formatting | bytes 147456 | tf_op jit(solution)/shard_map/all_to_all | solution.py:189
  118.7 15.4 %all_to_all.14 = f32[3,32,192]{2,0,1:T(4,128)S(1)} all-to-all(f32[3,32,192]{2,0,1:T(4,128)S(1)} %copy.25), channel_id=1, replica_groups=mesh['gx'=8,'gy'=4] {'gx','gy'}, dimensions={1} | all-to-all | bytes 147456 | tf_op jit(solution)/shard_map/all_to_all | solution.py:189
  134.9 1.1 add_select_fusion
  (75 shorter events, 8.0 us)
Async XLA Ops:
  0.6 22.7 %copy-start = (f32[8,32,2048]{2,1,0:T(8,128)S(1)}, f32[8,32,2048]{2,1,0:T(8,128)}, u32[]{:S(2)}) copy-start(f32[8,32,2048]{2,1,0:T(8,128)} %param.11) | copy-start | bytes 6291460
  0.6 19.0 %copy-start.5 = (s32[2048,1]{0,1:T(1,128)S(1)}, s32[2048,1]{0,1:T(1,128)}, u32[]{:S(2)}) copy-start(s32[2048,1]{0,1:T(1,128)} %param.19) | copy-start | bytes 24580
  0.7 19.2 %copy-start.7 = (s32[2048]{0:T(1024)S(1)}, s32[2048]{0:T(1024)}, u32[]{:S(2)}) copy-start(s32[2048]{0:T(1024)} %param.18) | copy-start | bytes 24580
  3.5 16.3 %collective-permute-start = (f32[8,3,2048]{2,1,0:T(4,128)S(1)}, f32[8,3,2048]{2,1,0:T(4,128)S(1)}, u32[]{:S(2)}, u32[]{:S(2)}) collective-permute-start(f32[8,3,2048]{2,1,0:T(4,128)S(1)} %pad_maximum_fusion.5), channel_id=1, source_target_pairs={{0,1},{1,2},{2,3},{3,4},{4,5},{5,6},{6,7},{7,8},{8,9},{9,10},{10,1... | collective-permute-start | bytes 589832 | tf_op jit(solution)/shard_map/ppermute | solution.py:21
  8.6 14.6 %collective-permute-start.1 = (f32[8,3,2048]{2,1,0:T(4,128)S(1)}, f32[8,3,2048]{2,1,0:T(4,128)S(1)}, u32[]{:S(2)}, u32[]{:S(2)}) collective-permute-start(f32[8,3,2048]{2,1,0:T(4,128)S(1)} %pad_maximum_fusion.6), channel_id=1, source_target_pairs={{1,0},{2,1},{3,2},{4,3},{5,4},{6,5},{7,6},{8,7},{9,8},{10,9},{11,1... | collective-permute-start | bytes 589832 | tf_op jit(solution)/shard_map/ppermute | solution.py:21
  10.7 41.2 %collective-permute-start.4 = (f32[2,3,512]{2,1,0:T(4,128)S(1)}, f32[2,3,512]{2,1,0:T(4,128)S(1)}, u32[]{:S(2)}, u32[]{:S(2)}) collective-permute-start(f32[2,3,512]{2,1,0:T(4,128)S(1)} %get-tuple-element.31), channel_id=1, source_target_pairs={{0,4},{4,8},{8,12},{12,16},{16,20},{20,24},{24,28},{1,5},{5,9},{9,... | collective-permute-start | bytes 36872 | tf_op jit(solution)/shard_map/ppermute | solution.py:21
  15.4 36.5 %collective-permute-start.5 = (f32[2,3,512]{2,1,0:T(4,128)S(1)}, f32[2,3,512]{2,1,0:T(4,128)S(1)}, u32[]{:S(2)}, u32[]{:S(2)}) collective-permute-start(f32[2,3,512]{2,1,0:T(4,128)S(1)} %get-tuple-element.32), channel_id=1, source_target_pairs={{4,0},{8,4},{12,8},{16,12},{20,16},{24,20},{28,24},{5,1},{9,5},{13... | collective-permute-start | bytes 36872 | tf_op jit(solution)/shard_map/ppermute | solution.py:21
  19.9 3.8 %copy-start.8 = (f32[7]{0:T(128)S(1)}, f32[7]{0:T(128)}, u32[]{:S(2)}) copy-start(f32[7]{0:T(128)} %param.14) | copy-start | bytes 88
  23.7 1.6 %copy-start.1 = (f32[8,32,2048]{2,1,0:T(8,128)S(1)}, f32[8,32,2048]{2,1,0:T(8,128)}, u32[]{:S(2)}) copy-start(f32[8,32,2048]{2,1,0:T(8,128)} %param.12) | copy-start | bytes 6291460
  23.8 1.6 %copy-start.9 = (f32[8]{0:T(128)S(1)}, f32[8]{0:T(128)}, u32[]{:S(2)}) copy-start(f32[8]{0:T(128)} %param.13) | copy-start | bytes 100
  35.9 4.2 %collective-permute-start.2 = (f32[2,2048]{1,0:T(2,128)S(1)}, f32[2,2048]{1,0:T(2,128)S(1)}, u32[]{:S(2)}, u32[]{:S(2)}) collective-permute-start(f32[2,2048]{1,0:T(2,128)S(1)} %get-tuple-element.33), channel_id=1, source_target_pairs={{0,1},{1,2},{2,3},{3,4},{4,5},{5,6},{6,7},{7,8},{8,9},{9,10},{10,1... | collective-permute-start | bytes 49160 | tf_op jit(solution)/shard_map/ppermute | solution.py:21
  38.4 5.6 %collective-permute-start.3 = (f32[2,2048]{1,0:T(2,128)S(1)}, f32[2,2048]{1,0:T(2,128)S(1)}, u32[]{:S(2)}, u32[]{:S(2)}) collective-permute-start(f32[2,2048]{1,0:T(2,128)S(1)} %get-tuple-element.34), channel_id=1, source_target_pairs={{1,0},{2,1},{3,2},{4,3},{5,4},{6,5},{7,6},{8,7},{9,8},{10,9},{11,1... | collective-permute-start | bytes 49160 | tf_op jit(solution)/shard_map/ppermute | solution.py:21
  44.2 7.7 %copy-start.2 = (f32[128,512]{1,0:T(8,128)S(1)}, f32[128,512]{1,0:T(8,128)}, u32[]{:S(2)}) copy-start(f32[128,512]{1,0:T(8,128)} %param.17) | copy-start | bytes 786436
  44.2 7.7 %copy-start.3 = (f32[128,512]{1,0:T(8,128)S(1)}, f32[128,512]{1,0:T(8,128)}, u32[]{:S(2)}) copy-start(f32[128,512]{1,0:T(8,128)} %param.16) | copy-start | bytes 786436
  46.5 24.8 %all-to-all-start = ((f32[4,2,36,516]{3,1,2,0:T(2,128)}), f32[4,2,36,516]{3,1,2,0:T(2,128)S(1)}, u32[]{:S(2)}, u32[]{:S(2)}) async-start(f32[4,2,36,516]{3,1,2,0:T(2,128)} %pad_maximum_fusion.1), calls=%async_computation | async-start | bytes 1474560 | tf_op jit(solution)/shard_map/all_to_all | solution.py:115
  52.1 14.6 %collective-permute-start.6 = (f32[2,134,3]{2,1,0:T(8,128)S(1)}, f32[2,134,3]{2,1,0:T(8,128)S(1)}, u32[]{:S(2)}, u32[]{:S(2)}) collective-permute-start(f32[2,134,3]{2,1,0:T(8,128)S(1)} %get-tuple-element.29), channel_id=1, source_target_pairs={{0,1},{1,2},{2,3},{4,5},{5,6},{6,7},{8,9},{9,10},{10,11},{12,13},{... | collective-permute-start | bytes 9656 | tf_op jit(solution)/shard_map/ppermute | solution.py:21
  56.0 10.7 %collective-permute-start.7 = (f32[2,134,3]{2,1,0:T(8,128)S(1)}, f32[2,134,3]{2,1,0:T(8,128)S(1)}, u32[]{:S(2)}, u32[]{:S(2)}) collective-permute-start(f32[2,134,3]{2,1,0:T(8,128)S(1)} %get-tuple-element.30), channel_id=1, source_target_pairs={{1,0},{2,1},{3,2},{5,4},{6,5},{7,6},{9,8},{10,9},{11,10},{13,12},{... | collective-permute-start | bytes 9656 | tf_op jit(solution)/shard_map/ppermute | solution.py:21
  117.2 17.7 %copy-start.4 = (f32[2,1,6144]{2,1,0:T(1,128)S(1)}, f32[2,1,6144]{2,1,0:T(1,128)}, u32[]{:S(2)}) copy-start(f32[2,1,6144]{2,1,0:T(1,128)} %param.20) | copy-start | bytes 147460
  117.2 17.7 %copy-start.6 = (f32[1,6144]{1,0:T(1,128)S(1)}, f32[1,6144]{1,0:T(1,128)}, u32[]{:S(2)}) copy-start(f32[1,6144]{1,0:T(1,128)} %param.21) | copy-start | bytes 73732
where the time goes:
time: 137 us
  local copies, waits for them, and re-layouts  51 us (37%)
  starting transfers between devices  26.7 us (19%)
  waiting for transfers between devices  20.8 us (15%)
  other arithmetic  20.7 us (15%)
  blocking collectives  15.4 us (11%)
    ppermute x8, starting transfers between devices, exchange(): return (lax.ppermute(last, axis, up), lax.ppermute(leading, axis, down))  21.4 us
    gather x1, local copies, waits for them, and re-layouts, body(): picked = fields[:, joint_cell]  18.2 us
    ppermute x8, waiting for transfers between devices, exchange(): return (lax.ppermute(last, axis, up), lax.ppermute(leading, axis, down))  16.5 us
    another operation x1, local copies, waits for them, and re-layouts, body(): fields = jnp.stack([(warp - warp_prev).reshape(-1), top.reshape(-1)])  15.6 us
    all_to_all x1, blocking collectives, body(): lax.all_to_all(outgoing, FLAT, split_axis=1, concat_axis=1, tiled=True)  15.4 us
    scatter x1, local copies, waits for them, and re-layouts, body(): jnp.zeros((3, devices * capacity), jnp.float32).at[:, slots].set(values)  6.81 us
    all_to_all x1, starting transfers between devices, relay(): recv = lax.all_to_all(send, 'gy', split_axis=0, concat_axis=0, tiled=True)  5.38 us
    add x1, other arithmetic, moment_of(): total = total + weighting[layer] * field[layer]  5.21 us
  transfers between devices with their start and end apart: 9, of which 4 were waited for; matrix products, arithmetic and copies ran while one was open for 14% of the time, Pallas kernels for 0%

commit v1 on v0

--- a/solution.py
+++ b/solution.py
@@ -186,7 +186,10 @@
     picked = fields[:, joint_cell]
     values = jnp.concatenate([picked, jnp.ones_like(picked[:1])], axis=0)
     outgoing = jnp.zeros((3, devices * capacity), jnp.float32).at[:, slots].set(values)
-    incoming = lax.all_to_all(outgoing, FLAT, split_axis=1, concat_axis=1, tiled=True)
+    incoming = jnp.concatenate(
+        lax.all_to_all(jnp.stack(jnp.split(outgoing, lax.axis_size(FLAT), axis=1)), FLAT, 0, 0),
+        axis=1,
+    )
     strain_next, resist_next = anand(joint_strain, joint_resist, incoming[:, None, :])
     return (warp, strain_next, resist_next)
 

time: 137 us -> 160 us (1.17)
  local copies, waits for them, and re-layouts: 51 us -> 72.9 us
    unnamed x22 -> x53, local copies, waits for them, and re-layouts: 1.59 us -> 21.6 us
    another operation x0 -> x2, local copies, waits for them, and re-layouts: none -> 3.31 us  [body(): jnp.stack(jnp.split(outgoing, lax.axis_size(FLAT), axis=1))]
  transfers between devices with their start and end apart: 9 -> 9, of which waited for: 4 -> 4; matrix products, arithmetic and copies ran while one was open for 14% -> 12% of each run, Pallas kernels for 0% -> 0%
where the time goes in v1:
time: 160 us; the launch traced here: 159 us
  local copies, waits for them, and re-layouts  72.9 us (46%)
  starting transfers between devices  27 us (17%)
  other arithmetic  21.3 us (13%)
  waiting for transfers between devices  20 us (12%)
  blocking collectives  15.7 us (10%)
    unnamed x53, local copies, waits for them, and re-layouts  21.6 us
    ppermute x8, starting transfers between devices, exchange(): return (lax.ppermute(last, axis, up), lax.ppermute(leading, axis, down))  21.4 us
    gather x1, local copies, waits for them, and re-layouts, body(): picked = fields[:, joint_cell]  18.2 us
    all_to_all x1, blocking collectives, body(): lax.all_to_all(jnp.stack(jnp.split(outgoing, lax.axis_size(FLAT), axis=1)...  15.7 us
    another operation x1, local copies, waits for them, and re-layouts, body(): fields = jnp.stack([(warp - warp_prev).reshape(-1), top.reshape(-1)])  15.6 us
    ppermute x8, waiting for transfers between devices, exchange(): return (lax.ppermute(last, axis, up), lax.ppermute(leading, axis, down))  15.6 us
    scatter x1, local copies, waits for them, and re-layouts, body(): jnp.zeros((3, devices * capacity), jnp.float32).at[:, slots].set(values)  6.81 us
    all_to_all x1, starting transfers between devices, relay(): recv = lax.all_to_all(send, 'gy', split_axis=0, concat_axis=0, tiled=True)  5.66 us
  transfers between devices with their start and end apart: 9, of which 4 were waited for; matrix products, arithmetic and copies ran while one was open for 12% of the time, Pallas kernels for 0%

profile of v1, /device:TPU:0, one launch (start us, length us, event | category | flops | bytes accessed | tf_op | source)
XLA Modules:
  0.0 159.2 jit_solution(2403248981146977094)
XLA Ops:
  0.7 1.4 fusion.120
  2.1 1.3 fusion.121
  3.5 5.0 %collective-permute-start = (f32[8,3,2048]{2,1,0:T(4,128)S(1)}, f32[8,3,2048]{2,1,0:T(4,128)S(1)}, u32[]{:S(2)}, u32[]{:S(2)}) collective-permute-start(f32[8,3,2048]{2,1,0:T(4,128)S(1)} %pad_maximum_fusion.5), channel_id=1, source_target_pairs={{0,1},{1,2},{2,3},{3,4},{4,5},{5,6},{6,7},{7,8},{8,9},{9,10},{10,1... | collective-permute-start | bytes 589832 | tf_op jit(solution)/shard_map/ppermute | solution.py:21
  8.6 1.3 collective-permute-start.1
  9.9 0.8 pad_maximum_fusion.14
  10.7 4.7 %collective-permute-start.4 = (f32[2,3,512]{2,1,0:T(4,128)S(1)}, f32[2,3,512]{2,1,0:T(4,128)S(1)}, u32[]{:S(2)}, u32[]{:S(2)}) collective-permute-start(f32[2,3,512]{2,1,0:T(4,128)S(1)} %get-tuple-element.31), channel_id=1, source_target_pairs={{0,4},{4,8},{8,12},{12,16},{16,20},{20,24},{24,28},{1,5},{5,9},{9,... | collective-permute-start | bytes 36872 | tf_op jit(solution)/shard_map/ppermute | solution.py:21
  15.4 1.3 collective-permute-start.5
  16.7 1.6 %fusion.126 = (f32[1]{0:T(128)}, f32[1]{0:T(128)}, f32[1]{0:T(128)}, f32[1]{0:T(128)}, f32[1]{0:T(128)}, /*index=5*/f32[1]{0:T(128)}, f32[1]{0:T(128)}, f32[1]{0:T(128)}) fusion(f32[8]{0:T(128)} %param.15), kind=kLoop, calls=%fused_computation.261 | loop fusion | bytes 64 | tf_op jit(solution)/shard_map/slice | solution.py:44
  18.3 0.9 convolution_bitcast_fusion
  19.6 0.9 select_reduce_fusion
  20.6 2.7 %collective-permute-done.1 = f32[8,3,2048]{2,1,0:T(4,128)S(1)} collective-permute-done((f32[8,3,2048]{2,1,0:T(4,128)S(1)}, f32[8,3,2048]{2,1,0:T(4,128)S(1)}, u32[]{:S(2)}, u32[]{:S(2)}) %collective-permute-start.1) | collective-permute-done | bytes 196640 | tf_op jit(solution)/shard_map/ppermute | solution.py:21
  24.3 1.0 copy-done.1
  25.3 3.0 %fusion.7 = f32[8,34,2048]{2,1,0:T(8,128)S(1)} fusion(f32[8,36,2048]{2,1,0:T(8,128)S(1)} %pad_maximum_fusion, f32[8,2,2048]{2,1,0:T(2,128)S(1)} %slice.391, f32[8,32,2048]{2,1,0:T(8,128)S(1)} %copy-done, f32[8,2,2048]{2,1,0:T(2,128)S(1)} %slice.390, f32[8,1,2048]{2,1,0:T(1,128)S(1)} %slice.396, f32[8,32,2048]{2,1,0:T(8,128)S(1)} %copy-done.1, ...), kind=kLoop, calls=%fused_computation.13 | loop fusion | flops 8355840 | bytes 14353408 | tf_op jit(solution)/shard_map/jit(_where)/select_n | solution.py:101
  28.8 1.9 %fusion.15 = f32[8,32,2048]{2,1,0:T(8,128)S(1)} fusion(f32[8,32,2048]{2,1,0:T(8,128)S(1)} %copy-done.1, f32[8,34,2048]{2,1,0:T(8,128)S(1)} %fusion.7, f32[7,32,2048]{2,1,0:T(8,128)S(1)} %fusion.16, f32[8]{0:T(128)S(1)} %copy-done.9), kind=kLoop, calls=%fused_computation.24 | loop fusion | flops 5242880 | bytes 14942720 | tf_op jit(solution)/shard_map/add | solution.py:40
  30.7 5.2 %fusion.54 = f32[32,2048]{1,0:T(8,128)S(1)} fusion(f32[8,32,2048]{2,1,0:T(8,128)S(1)} %fusion.15, f32[]{:T(128)} %bitcast.8, f32[]{:T(128)} %bitcast.6, f32[]{:T(128)} %bitcast.5, f32[]{:T(128)} %bitcast.4, f32[]{:T(128)} %bitcast.3, f32[]{:T(128)} %bitcast.2, f32[]{:T(128)} %bitcast.1, f32[]{:T(128)} %bitcast), kind=kLoop, calls=%fused_computation.109 | loop fusion | flops 983040 | bytes 2359328 | tf_op jit(solution)/shard_map/add | solution.py:46
  35.9 2.5 %collective-permute-start.2 = (f32[2,2048]{1,0:T(2,128)S(1)}, f32[2,2048]{1,0:T(2,128)S(1)}, u32[]{:S(2)}, u32[]{:S(2)}) collective-permute-start(f32[2,2048]{1,0:T(2,128)S(1)} %get-tuple-element.33), channel_id=1, source_target_pairs={{0,1},{1,2},{2,3},{3,4},{4,5},{5,6},{6,7},{7,8},{8,9},{9,10},{10,1... | collective-permute-start | bytes 49160 | tf_op jit(solution)/shard_map/ppermute | solution.py:21
  38.4 1.3 collective-permute-start.3
  40.2 3.9 %collective-permute-done.3 = f32[2,2048]{1,0:T(2,128)S(1)} collective-permute-done((f32[2,2048]{1,0:T(2,128)S(1)}, f32[2,2048]{1,0:T(2,128)S(1)}, u32[]{:S(2)}, u32[]{:S(2)}) %collective-permute-start.3) | collective-permute-done | bytes 16416 | tf_op jit(solution)/shard_map/ppermute | solution.py:21
  45.3 1.2 pad_maximum_fusion.1
  46.5 5.7 %all-to-all-start = ((f32[4,2,36,516]{3,1,2,0:T(2,128)}), f32[4,2,36,516]{3,1,2,0:T(2,128)S(1)}, u32[]{:S(2)}, u32[]{:S(2)}) async-start(f32[4,2,36,516]{3,1,2,0:T(2,128)} %pad_maximum_fusion.1), calls=%async_computation | async-start | bytes 1474560 | tf_op jit(solution)/shard_map/all_to_all | solution.py:115
  52.3 3.9 %collective-permute-start.6 = (f32[2,134,3]{2,1,0:T(8,128)S(1)}, f32[2,134,3]{2,1,0:T(8,128)S(1)}, u32[]{:S(2)}, u32[]{:S(2)}) collective-permute-start(f32[2,134,3]{2,1,0:T(8,128)S(1)} %get-tuple-element.29), channel_id=1, source_target_pairs={{0,1},{1,2},{2,3},{4,5},{5,6},{6,7},{8,9},{9,10},{10,11},{12,13},{... | collective-permute-start | bytes 9656 | tf_op jit(solution)/shard_map/ppermute | solution.py:21
  56.3 1.5 collective-permute-start.7
  57.8 9.0 %collective-permute-done.6 = f32[2,134,3]{2,1,0:T(8,128)S(1)} collective-permute-done((f32[2,134,3]{2,1,0:T(8,128)S(1)}, f32[2,134,3]{2,1,0:T(8,128)S(1)}, u32[]{:S(2)}, u32[]{:S(2)}) %collective-permute-start.6) | collective-permute-done | bytes 3248 | tf_op jit(solution)/shard_map/ppermute | solution.py:21
  67.2 4.4 %all-to-all-done = f32[4,2,36,516]{3,1,2,0:T(2,128)S(1)} async-done(((f32[4,2,36,516]{3,1,2,0:T(2,128)}), f32[4,2,36,516]{3,1,2,0:T(2,128)S(1)}, u32[]{:S(2)}, u32[]{:S(2)}) %all-to-all-start) | async-done | bytes 594464 | tf_op jit(solution)/shard_map/all_to_all | solution.py:115
  73.8 0.9 fusion.23
  74.7 1.4 subtract_bitcast_fusion
  76.9 15.6 %copy.64 = f32[2,65536]{0,1:T(8,128)} copy(f32[2,65536]{1,0:T(2,128)S(1)} %pad_maximum_fusion.3) | data formatting | bytes 1048576 | tf_op jit(solution)/shard_map/stack | solution.py:185
  92.5 18.2 %gather_fusion = f32[2048,2]{1,0:T(8,128)} fusion(f32[2,65536]{0,1:T(8,128)} %copy.64, s32[2048]{0:T(1024)S(1)} %fusion.111), kind=kCustom, calls=%fused_computation | custom fusion | bytes 40960 | tf_op jit(solution)/shard_map/gather | solution.py:186
  110.7 6.8 %scatter_custom_fusion = f32[3,6144]{0,1:T(8,128)S(1)} fusion(s32[2048]{0:T(1024)S(1)} %bitcast.231, f32[]{:T(128)} %constant.34.clone.1, f32[2,2048]{0,1:T(8,128)} %bitcast.223, f32[]{:T(128)} %constant.45.clone.1), kind=kCustom, calls=%fused_computation.28 | custom fusion | bytes 90120 | tf_op jit(solution)/shard_map/scatter | solution.py:188
  138.2 2.7 %copy.65 = f32[32,3,192]{2,1,0:T(4,128)S(1)} copy(f32[32,3,192]{1,2,0:T(8,128)} %fusion.68) | data formatting | bytes 147456 | tf_op jit(solution)/shard_map/stack | solution.py:190
  140.8 15.7 %all_to_all.10 = f32[32,3,192]{2,1,0:T(4,128)S(1)} all-to-all(f32[32,3,192]{2,1,0:T(4,128)S(1)} %copy.65), channel_id=1, replica_groups=mesh['gx'=8,'gy'=4] {'gx','gy'}, dimensions={0} | all-to-all | bytes 147456 | tf_op jit(solution)/shard_map/all_to_all | solution.py:190
  157.3 1.1 add_select_fusion
  (107 shorter events, 29.3 us)
Async XLA Ops:
  0.6 22.7 %copy-start = (f32[8,32,2048]{2,1,0:T(8,128)S(1)}, f32[8,32,2048]{2,1,0:T(8,128)}, u32[]{:S(2)}) copy-start(f32[8,32,2048]{2,1,0:T(8,128)} %param.11) | copy-start | bytes 6291460
  0.6 19.9 %copy-start.5 = (s32[2048,1]{0,1:T(1,128)S(1)}, s32[2048,1]{0,1:T(1,128)}, u32[]{:S(2)}) copy-start(s32[2048,1]{0,1:T(1,128)} %param.19) | copy-start | bytes 24580
  0.7 19.9 %copy-start.7 = (s32[2048]{0:T(1024)S(1)}, s32[2048]{0:T(1024)}, u32[]{:S(2)}) copy-start(s32[2048]{0:T(1024)} %param.18) | copy-start | bytes 24580
  3.5 17.0 %collective-permute-start = (f32[8,3,2048]{2,1,0:T(4,128)S(1)}, f32[8,3,2048]{2,1,0:T(4,128)S(1)}, u32[]{:S(2)}, u32[]{:S(2)}) collective-permute-start(f32[8,3,2048]{2,1,0:T(4,128)S(1)} %pad_maximum_fusion.5), channel_id=1, source_target_pairs={{0,1},{1,2},{2,3},{3,4},{4,5},{5,6},{6,7},{7,8},{8,9},{9,10},{10,1... | collective-permute-start | bytes 589832 | tf_op jit(solution)/shard_map/ppermute | solution.py:21
  8.6 14.6 %collective-permute-start.1 = (f32[8,3,2048]{2,1,0:T(4,128)S(1)}, f32[8,3,2048]{2,1,0:T(4,128)S(1)}, u32[]{:S(2)}, u32[]{:S(2)}) collective-permute-start(f32[8,3,2048]{2,1,0:T(4,128)S(1)} %pad_maximum_fusion.6), channel_id=1, source_target_pairs={{1,0},{2,1},{3,2},{4,3},{5,4},{6,5},{7,6},{8,7},{9,8},{10,9},{11,1... | collective-permute-start | bytes 589832 | tf_op jit(solution)/shard_map/ppermute | solution.py:21
  10.7 41.5 %collective-permute-start.4 = (f32[2,3,512]{2,1,0:T(4,128)S(1)}, f32[2,3,512]{2,1,0:T(4,128)S(1)}, u32[]{:S(2)}, u32[]{:S(2)}) collective-permute-start(f32[2,3,512]{2,1,0:T(4,128)S(1)} %get-tuple-element.31), channel_id=1, source_target_pairs={{0,4},{4,8},{8,12},{12,16},{16,20},{20,24},{24,28},{1,5},{5,9},{9,... | collective-permute-start | bytes 36872 | tf_op jit(solution)/shard_map/ppermute | solution.py:21
  15.4 36.8 %collective-permute-start.5 = (f32[2,3,512]{2,1,0:T(4,128)S(1)}, f32[2,3,512]{2,1,0:T(4,128)S(1)}, u32[]{:S(2)}, u32[]{:S(2)}) collective-permute-start(f32[2,3,512]{2,1,0:T(4,128)S(1)} %get-tuple-element.32), channel_id=1, source_target_pairs={{4,0},{8,4},{12,8},{16,12},{20,16},{24,20},{28,24},{5,1},{9,5},{13... | collective-permute-start | bytes 36872 | tf_op jit(solution)/shard_map/ppermute | solution.py:21
  18.3 5.4 %copy-start.8 = (f32[7]{0:T(128)S(1)}, f32[7]{0:T(128)}, u32[]{:S(2)}) copy-start(f32[7]{0:T(128)} %param.14) | copy-start | bytes 88
  23.7 1.6 %copy-start.1 = (f32[8,32,2048]{2,1,0:T(8,128)S(1)}, f32[8,32,2048]{2,1,0:T(8,128)}, u32[]{:S(2)}) copy-start(f32[8,32,2048]{2,1,0:T(8,128)} %param.12) | copy-start | bytes 6291460
  23.8 1.6 copy-start.9
  35.9 4.2 %collective-permute-start.2 = (f32[2,2048]{1,0:T(2,128)S(1)}, f32[2,2048]{1,0:T(2,128)S(1)}, u32[]{:S(2)}, u32[]{:S(2)}) collective-permute-start(f32[2,2048]{1,0:T(2,128)S(1)} %get-tuple-element.33), channel_id=1, source_target_pairs={{0,1},{1,2},{2,3},{3,4},{4,5},{5,6},{6,7},{7,8},{8,9},{9,10},{10,1... | collective-permute-start | bytes 49160 | tf_op jit(solution)/shard_map/ppermute | solution.py:21
  38.4 5.6 %collective-permute-start.3 = (f32[2,2048]{1,0:T(2,128)S(1)}, f32[2,2048]{1,0:T(2,128)S(1)}, u32[]{:S(2)}, u32[]{:S(2)}) collective-permute-start(f32[2,2048]{1,0:T(2,128)S(1)} %get-tuple-element.34), channel_id=1, source_target_pairs={{1,0},{2,1},{3,2},{4,3},{5,4},{6,5},{7,6},{8,7},{9,8},{10,9},{11,1... | collective-permute-start | bytes 49160 | tf_op jit(solution)/shard_map/ppermute | solution.py:21
  39.9 12.3 %copy-start.2 = (f32[128,512]{1,0:T(8,128)S(1)}, f32[128,512]{1,0:T(8,128)}, u32[]{:S(2)}) copy-start(f32[128,512]{1,0:T(8,128)} %param.17) | copy-start | bytes 786436
  39.9 12.3 %copy-start.3 = (f32[128,512]{1,0:T(8,128)S(1)}, f32[128,512]{1,0:T(8,128)}, u32[]{:S(2)}) copy-start(f32[128,512]{1,0:T(8,128)} %param.16) | copy-start | bytes 786436
  46.5 25.1 %all-to-all-start = ((f32[4,2,36,516]{3,1,2,0:T(2,128)}), f32[4,2,36,516]{3,1,2,0:T(2,128)S(1)}, u32[]{:S(2)}, u32[]{:S(2)}) async-start(f32[4,2,36,516]{3,1,2,0:T(2,128)} %pad_maximum_fusion.1), calls=%async_computation | async-start | bytes 1474560 | tf_op jit(solution)/shard_map/all_to_all | solution.py:115
  52.3 14.5 %collective-permute-start.6 = (f32[2,134,3]{2,1,0:T(8,128)S(1)}, f32[2,134,3]{2,1,0:T(8,128)S(1)}, u32[]{:S(2)}, u32[]{:S(2)}) collective-permute-start(f32[2,134,3]{2,1,0:T(8,128)S(1)} %get-tuple-element.29), channel_id=1, source_target_pairs={{0,1},{1,2},{2,3},{4,5},{5,6},{6,7},{8,9},{9,10},{10,11},{12,13},{... | collective-permute-start | bytes 9656 | tf_op jit(solution)/shard_map/ppermute | solution.py:21
  56.3 10.5 %collective-permute-start.7 = (f32[2,134,3]{2,1,0:T(8,128)S(1)}, f32[2,134,3]{2,1,0:T(8,128)S(1)}, u32[]{:S(2)}, u32[]{:S(2)}) collective-permute-start(f32[2,134,3]{2,1,0:T(8,128)S(1)} %get-tuple-element.30), channel_id=1, source_target_pairs={{1,0},{2,1},{3,2},{5,4},{6,5},{7,6},{9,8},{10,9},{11,10},{13,12},{... | collective-permute-start | bytes 9656 | tf_op jit(solution)/shard_map/ppermute | solution.py:21
  130.4 26.9 %copy-start.4 = (f32[2,1,6144]{2,1,0:T(1,128)S(1)}, f32[2,1,6144]{2,1,0:T(1,128)}, u32[]{:S(2)}) copy-start(f32[2,1,6144]{2,1,0:T(1,128)} %param.20) | copy-start | bytes 147460
  130.4 26.9 %copy-start.6 = (f32[1,6144]{1,0:T(1,128)S(1)}, f32[1,6144]{1,0:T(1,128)}, u32[]{:S(2)}) copy-start(f32[1,6144]{1,0:T(1,128)} %param.21) | copy-start | bytes 73732
